TPU v7x, 32 devices: a whole 2x2x4 slice. The times are simulated.
32 devices in a mesh: seq: 8 (over z, x), tp: 4 (over y, core).
Axes of the slice: x: 2, y: 2, z: 4, core: 2. Of those that a mesh axis runs over, the one named last changes fastest.
Arguments:
- hidden: bfloat16 [2048, 2048], P('seq', 'tp'), may hold values from -40 to 40
- new_queries: bfloat16 [2048, 2048], P('seq', 'tp'), may hold values from -9 to 9
- new_keys: bfloat16 [2048, 2048], P('seq', 'tp'), may hold values from -6 to 6
- new_values: bfloat16 [2048, 2048], P('seq', 'tp'), may hold values from -6 to 6
- cache_keys: bfloat16 [8, 4096, 2048], P('seq', None, 'tp'), may hold values from -6 to 6
- cache_values: bfloat16 [8, 4096, 2048], P('seq', None, 'tp'), may hold values from -6 to 6
- cache_lengths: int32 [8], replicated, may hold values from 1 to 4096, as said below
- out_proj: bfloat16 [2048, 2048], P('tp'), may hold values from -0.5 to 0.5
- moe_gain: float32 [2048], P('tp'), may hold values from 0.1 to 1.9
- expert_ids: int32 [2048, 8], P('seq'), may hold values from 0 to 15, all different within a row; in each aligned block of 256 rows (0 to 255, 256 to 511, ...) at most 192 rows name the same one
- route_weights: float32 [2048, 8], P('seq'), may hold values from 0.25 to 0.5
- expert_gate_up: bfloat16 [16, 2048, 2, 1024], P('seq', None, None, 'tp'), may hold values from -0.125 to 0.125
- expert_down: bfloat16 [16, 1024, 2048], P('seq', 'tp'), may hold values from -0.375 to 0.375
- next_gain: float32 [2048], P('tp'), may hold values from 0.1 to 1.9
- qkv_proj: bfloat16 [2048, 3, 2048], P(None, None, 'tp'), may hold values from -0.125 to 0.125
- query_gain: float32 [2048], P('tp'), may hold values from 0.1 to 1.9
- key_gain: float32 [2048], P('tp'), may hold values from 0.1 to 1.9
Outputs:
- layer_out: bfloat16 [2048, 2048], P('seq', 'tp')
- next_query: bfloat16 [2048, 2048], P('seq', 'tp')
- next_key: bfloat16 [2048, 2048], P('seq', 'tp')
- next_value: bfloat16 [2048, 2048], P('seq', 'tp')
Inputs may be any that keep to these rules, and one draw needn't show every extreme that they name: Request r has cached positions 0 to cache_lengths[r] - 1; one request has 4096 of them and one has 1. `expert_ids`: each row names 8 different experts; among the 256 rows of one request no expert is named more than 192 times, and in some request one expert is named exactly 192 times.
All inputs are finite; a program needn't handle non-finite values.
Results may differ from a plain program's by a relative error of at most 0.017.
Values may be sent and summed in bfloat16 or wider, within the bound.
No kernel may reach another device: no remote copies, remote signals or barrier semaphores. Data moves between devices by JAX's collectives and lax.ppermute only.
A program may use at most 128 MiB of HBM per device.

v0:
```python
import math
import jax
import jax.numpy as jnp
from jax import lax
from jax.sharding import PartitionSpec as P

D = 2048
HEAD_DIM = 128
TOP = 8
NEW = 256
epsilon = 1e-05


def softmax_parts(queries, key_rows, values, allowed):
    scores = jnp.einsum(
        "bthe,bche->bhtc", queries, key_rows, preferred_element_type=jnp.float32
    ) / math.sqrt(HEAD_DIM)
    scores = jnp.where(allowed[:, None], scores, -1e30)
    row_max = jnp.max(scores, axis=3)
    weights = jnp.where(allowed[:, None], jnp.exp(scores - row_max[..., None]), 0.0)
    row_total = jnp.sum(weights, axis=3)
    partial_out = jnp.einsum(
        "bhtc,bche->bthe", weights.astype(jnp.bfloat16), values, preferred_element_type=jnp.float32
    )
    return (partial_out, jnp.swapaxes(row_max, 1, 2), jnp.swapaxes(row_total, 1, 2))


def combine_parts(first, second):
    out_a, max_a, total_a = first
    out_b, max_b, total_b = second
    joint = jnp.maximum(max_a, max_b)
    factor_a = jnp.exp(max_a - joint)
    factor_b = jnp.exp(max_b - joint)
    return (
        out_a * factor_a[..., None] + out_b * factor_b[..., None],
        joint,
        total_a * factor_a + total_b * factor_b,
    )


def merge_parts(pieces, maxima, totals):
    overall = jnp.max(maxima, axis=0)
    factor = jnp.exp(maxima - overall[None])
    denominator = jnp.sum(totals * factor, axis=0)
    merged = jnp.sum(pieces * factor[..., None], axis=0)
    return merged / denominator[..., None]


def dense_experts(moe_in, expert_ids, route_weights, expert_gate_up, down_full, here, experts_all):
    local_experts = expert_gate_up.shape[0]
    hidden_quarter = expert_gate_up.shape[3]
    tokens, quarter = moe_in.shape
    seq_count = experts_all // local_experts
    gate_w = jnp.sum(
        route_weights[:, :, None]
        * (expert_ids[:, :, None] == jnp.arange(experts_all, dtype=jnp.int32)[None, None, :]),
        axis=1,
    )
    gate_t = jnp.transpose(gate_w)
    gate_hi = gate_t.astype(jnp.bfloat16)
    gate_lo = (gate_t - gate_hi.astype(jnp.float32)).astype(jnp.bfloat16)
    info = jnp.concatenate([gate_hi, gate_lo], axis=0).reshape(-1, quarter)
    packed = jnp.concatenate([moe_in, info], axis=0)
    gathered = lax.all_gather(packed, "seq", axis=0, tiled=False)
    rows_q = gathered[:, :tokens].reshape(seq_count * tokens, quarter)
    info_all = gathered[:, tokens:].reshape(seq_count, 2, experts_all, tokens).astype(jnp.float32)
    gate_all = info_all[:, 0] + info_all[:, 1]
    gate_local = lax.dynamic_slice_in_dim(gate_all, here * local_experts, local_experts, axis=1)
    gate_local = jnp.transpose(gate_local, (1, 0, 2)).reshape(local_experts, seq_count * tokens)
    rows = lax.all_gather(rows_q, "tp", axis=1, tiled=True)
    gate_up = expert_gate_up.reshape(local_experts, D, 2 * hidden_quarter)
    projected = jnp.einsum("td,edf->etf", rows, gate_up, preferred_element_type=jnp.float32)
    activated = jax.nn.silu(projected[..., :hidden_quarter]) * projected[..., hidden_quarter:]
    activated = activated.astype(jnp.bfloat16).astype(jnp.float32)
    weighted = (activated * gate_local[:, :, None]).astype(jnp.bfloat16)
    weighted = lax.all_gather(weighted, "tp", axis=2, tiled=True)
    partial = jnp.einsum(
        "etf,efd->td", weighted, down_full, preferred_element_type=jnp.float32
    ).astype(jnp.bfloat16)
    partial = lax.psum_scatter(partial, "seq", scatter_dimension=0, tiled=True)
    return partial.astype(jnp.float32)


def dispatch_experts(
    moe_in, expert_ids, route_weights, expert_gate_up, expert_down, experts_all, capacity
):
    quarter = moe_in.shape[1]
    local_experts = expert_gate_up.shape[0]
    flat_ids = expert_ids.reshape(NEW * TOP)
    onehot = (flat_ids[:, None] == jnp.arange(experts_all, dtype=jnp.int32)[None, :]).astype(
        jnp.int32
    )
    ranks = jnp.sum((jnp.cumsum(onehot, axis=0) - onehot) * onehot, axis=1)
    target = (flat_ids * capacity + ranks).reshape(NEW, TOP)
    slot_ids = jnp.arange(experts_all * capacity, dtype=jnp.int32)
    selector = jnp.sum(
        (target[None, :, :] == slot_ids[:, None, None]).astype(jnp.int32), axis=2
    ).astype(jnp.bfloat16)
    send_rows = jnp.dot(selector, moe_in, preferred_element_type=jnp.float32).astype(jnp.bfloat16)
    send_rows = send_rows.reshape(experts_all, capacity, quarter)
    received = lax.all_to_all(send_rows, "seq", split_axis=0, concat_axis=1, tiled=True)
    hidden_quarter = expert_gate_up.shape[3]
    gate_up_local = expert_gate_up.reshape(local_experts, D, 2 * hidden_quarter)
    weight_rows = gate_up_local
    projected = jnp.einsum(
        "erd,edf->erf",
        lax.all_gather(received, "tp", axis=2, tiled=True),
        weight_rows,
        preferred_element_type=jnp.float32,
    )
    activated = (
        jax.nn.silu(projected[..., :hidden_quarter]) * projected[..., hidden_quarter:]
    ).astype(jnp.bfloat16)
    down_terms = jnp.einsum(
        "erf,efd->erd", activated, expert_down, preferred_element_type=jnp.float32
    )
    expert_result = lax.psum_scatter(
        down_terms.astype(jnp.bfloat16), "tp", scatter_dimension=2, tiled=True
    )
    returned = lax.all_to_all(
        expert_result, "seq", split_axis=1, concat_axis=0, tiled=True
    ).reshape(experts_all * capacity, quarter)
    picked = jnp.take(returned, target, axis=0)
    return jnp.sum(route_weights[:, :, None] * picked.astype(jnp.float32), axis=1)


def body(
    hidden,
    new_queries,
    new_keys,
    new_values,
    cache_keys,
    cache_values,
    cache_lengths,
    out_proj,
    moe_gain,
    expert_ids,
    route_weights,
    expert_gate_up,
    expert_down,
    next_gain,
    qkv_proj,
    query_gain,
    key_gain,
):
    seq_count = lax.axis_size("seq")
    here = lax.axis_index("seq")
    local_experts = expert_gate_up.shape[0]
    experts_all = local_experts * seq_count
    capacity = max(2, 3 * NEW * TOP // (2 * experts_all))
    dense = NEW <= 2 * capacity
    if dense:
        tp_here = lax.axis_index("tp")
        quarter_width = hidden.shape[1]
        down_full = lax.all_gather(expert_down, "tp", axis=1, tiled=True)
        down_full = lax.dynamic_slice_in_dim(
            down_full, tp_here * quarter_width, quarter_width, axis=2
        )
    local_width = new_queries.shape[1]
    local_heads = local_width // HEAD_DIM
    quarter = hidden.shape[1]
    own_queries = new_queries.reshape(1, NEW, local_heads, HEAD_DIM)
    own_keys = new_keys.reshape(1, NEW, local_heads, HEAD_DIM)
    own_values = new_values.reshape(1, NEW, local_heads, HEAD_DIM)
    offsets = jnp.arange(NEW, dtype=jnp.int32)
    causal = (offsets[None, :] <= offsets[:, None])[None]
    own_out, own_max, own_total = softmax_parts(own_queries, own_keys, own_values, causal)
    span = cache_keys.shape[1]
    block = min(512, span)
    my_length = lax.dynamic_index_in_dim(cache_lengths, here, 0, keepdims=False)
    block_count = (my_length + block - 1) // block
    key_blocks = cache_keys.reshape(span, local_heads, HEAD_DIM)
    value_blocks = cache_values.reshape(span, local_heads, HEAD_DIM)

    def cache_block(index, carry):
        begin = index * block
        keys_here = lax.dynamic_slice_in_dim(key_blocks, begin, block, 0)[None]
        values_here = lax.dynamic_slice_in_dim(value_blocks, begin, block, 0)[None]
        positions = begin + jnp.arange(block, dtype=jnp.int32)
        allowed = jnp.broadcast_to((positions < my_length)[None, None, :], (1, NEW, block))
        return combine_parts(carry, softmax_parts(own_queries, keys_here, values_here, allowed))

    start_parts = (
        jnp.zeros((1, NEW, local_heads, HEAD_DIM), jnp.float32),
        jnp.full((1, NEW, local_heads), -1e30, jnp.float32),
        jnp.zeros((1, NEW, local_heads), jnp.float32),
    )
    pieces, maxima, totals = lax.fori_loop(0, block_count, cache_block, start_parts)
    attended = merge_parts(
        jnp.concatenate([own_out, pieces], 0),
        jnp.concatenate([own_max, maxima], 0),
        jnp.concatenate([own_total, totals], 0),
    )
    attended = attended.reshape(NEW, local_width).astype(jnp.bfloat16)
    if dense:
        attended, down_full = lax.optimization_barrier((attended, down_full))
    attn_term = jnp.dot(attended, out_proj, preferred_element_type=jnp.float32)
    residual = hidden.astype(jnp.float32) + lax.psum_scatter(
        attn_term.astype(jnp.bfloat16), "tp", scatter_dimension=1, tiled=True
    ).astype(jnp.float32)
    square_total = lax.psum(jnp.sum(residual * residual, axis=1), "tp")
    moe_in = (residual * lax.rsqrt(square_total / D + epsilon)[:, None] * moe_gain[None, :]).astype(
        jnp.bfloat16
    )
    if dense:
        moe_term = dense_experts(
            moe_in, expert_ids, route_weights, expert_gate_up, down_full, here, experts_all
        )
    else:
        moe_term = dispatch_experts(
            moe_in, expert_ids, route_weights, expert_gate_up, expert_down, experts_all, capacity
        )
    routed = residual + moe_term
    layer_out = routed.astype(jnp.bfloat16)
    scaled = (routed * next_gain[None, :]).astype(jnp.bfloat16)
    qkv_local = qkv_proj.reshape(D, 3 * local_width)
    weight_rows = qkv_local
    mixed = jnp.dot(
        lax.all_gather(scaled, "tp", axis=1, tiled=True),
        weight_rows,
        preferred_element_type=jnp.float32,
    )
    mixed = mixed.reshape(NEW, 3, local_width)
    squares_routed = jnp.sum(routed * routed, axis=1)
    routed_total, query_raw, key_raw = lax.psum(
        (
            squares_routed,
            jnp.sum(mixed[:, 0] * mixed[:, 0], axis=1),
            jnp.sum(mixed[:, 1] * mixed[:, 1], axis=1),
        ),
        "tp",
    )
    x_scale = lax.rsqrt(routed_total / D + epsilon)
    query_pre = mixed[:, 0] * x_scale[:, None]
    key_pre = mixed[:, 1] * x_scale[:, None]
    query_total = query_raw * x_scale * x_scale
    key_total = key_raw * x_scale * x_scale
    next_query = (
        query_pre * lax.rsqrt(query_total / D + epsilon)[:, None] * query_gain[None, :]
    ).astype(jnp.bfloat16)
    next_key = (key_pre * lax.rsqrt(key_total / D + epsilon)[:, None] * key_gain[None, :]).astype(
        jnp.bfloat16
    )
    next_value = (mixed[:, 2] * x_scale[:, None]).astype(jnp.bfloat16)
    return (layer_out, next_query, next_key, next_value)


def solution(mesh):
    return jax.shard_map(
        body,
        mesh=mesh,
        in_specs=(
            P("seq", "tp"),
            P("seq", "tp"),
            P("seq", "tp"),
            P("seq", "tp"),
            P("seq", None, "tp"),
            P("seq", None, "tp"),
            P(),
            P("tp", None),
            P("tp"),
            P("seq", None),
            P("seq", None),
            P("seq", None, None, "tp"),
            P("seq", "tp", None),
            P("tp"),
            P(None, None, "tp"),
            P("tp"),
            P("tp"),
        ),
        out_specs=(P("seq", "tp"), P("seq", "tp"), P("seq", "tp"), P("seq", "tp")),
        check_vma=False,
    )
```

profile of v0, /device:TPU:0, one launch (start us, length us, event | category | flops | bytes accessed | tf_op | source)
XLA Modules:
  0.0 412.0 jit_solution(3361592434585957795)
XLA Ops:
  7.2 0.7 all-gather.7.cloned.1.call-update
  9.6 6.4 %copy.95 = bf16[1,4096,512]{1,2,0:T(8,128)(2,1)} copy(bf16[1,4096,512]{2,1,0:T(8,128)(2,1)} %param.23) | data formatting | bytes 8388608 | tf_op args[4]
  16.0 6.6 %copy.97 = bf16[1,4096,512]{1,2,0:T(8,128)(2,1)} copy(bf16[1,4096,512]{2,1,0:T(8,128)(2,1)} %param.24) | data formatting | bytes 8388608 | tf_op args[5]
  22.7 28.9 %while.14 = (s32[]{:T(128)}, f32[1,256,4,128]{1,3,2,0:T(8,128)S(1)}, f32[1,256,4]{1,2,0:T(4,128)S(1)}, f32[1,256,4]{1,2,0:T(4,128)S(1)}, s32[]{:T(128)}, /*index...) while((s32[]{:T(128)}, ...), condition=%wide.region_4.5_spmd, body=%wide.region_1.4_spmd.sunk | while | flops 275651584 | bytes 8731323 | solution.py:188
  22.7 0.7 add_compare_fusion.2
  23.4 1.7 bitcast_reduce_fusion.2
  25.7 1.8 fusion.83
  27.6 0.7 add_compare_fusion.2
  28.2 1.6 bitcast_reduce_fusion.2
  30.5 1.8 fusion.83
  32.4 0.7 add_compare_fusion.2
  33.0 1.6 bitcast_reduce_fusion.2
  35.3 1.8 fusion.83
  37.2 0.7 add_compare_fusion.2
  37.8 1.6 bitcast_reduce_fusion.2
  40.1 1.8 fusion.83
  42.0 0.7 add_compare_fusion.2
  42.6 1.6 bitcast_reduce_fusion.2
  44.9 1.8 fusion.83
  46.8 0.7 add_compare_fusion.2
  47.4 1.6 bitcast_reduce_fusion.2
  49.7 1.8 fusion.83
  51.8 1.3 fusion.63
  54.5 16.1 %all-gather.7.cloned.1.call-done = bf16[2,1024,2048]{2,1,0:T(8,128)(2,1)} async-done(((bf16[2,256,2048]{2,1,0:T(8,128)(2,1)}), bf16[2,1024,2048]{2,1,0:T(8,128)(2,1)}) %all-gather.7.cloned.1.call-update) | async-done | bytes 8388624 | tf_op jit(solution)/shard_map/all_gather | solution.py:155
  70.6 3.0 constant_dynamic-slice_fusion
  73.7 1.7 convolution_convert_fusion
  75.5 24.9 %reduce-scatter.3.cloned.1.call-done = bf16[256,512]{1,0:T(8,128)(2,1)} async-done(((bf16[256,2048]{1,0:T(8,128)(2,1)}), bf16[256,512]{1,0:T(8,128)(2,1)}) %reduce-scatter.3.cloned.1.call-update) | async-done | bytes 262160 | tf_op jit(solution)/shard_map/reduce_scatter | solution.py:198
  100.4 1.1 multiply_reduce_fusion.3
  101.6 5.8 %psum.28 = f32[256]{0:T(256)S(1)} all-reduce(f32[256]{0:T(256)S(1)} %multiply_reduce_fusion.3), channel_id=1, replica_groups=mesh['seq'=8,'tp'=4] {'tp'}, use_global_device_ids=true, to_apply=%region_10.11 | all-reduce | flops 256 | bytes 2048 | tf_op jit(solution)/shard_map/psum | solution.py:201
  107.3 1.1 multiply_convert_fusion.4
  108.4 0.7 pad_maximum_fusion
  109.2 51.9 %all-gather.15.cloned.1.call-done = bf16[2176,512]{1,0:T(8,128)(2,1)} async-done(((bf16[272,512]{1,0:T(8,128)(2,1)}), bf16[2176,512]{1,0:T(8,128)(2,1)}) %all-gather.15.cloned.1.call-update) | async-done | bytes 2228240 | tf_op jit(solution)/shard_map/all_gather | solution.py:64
  161.1 3.1 slice.40
  164.2 7.8 %reshape.166 = bf16[2,2048,512]{2,1,0:T(8,128)(2,1)} reshape(bf16[2,2048,2,256]{3,2,1,0:T(2,128)(2,1)} %param.30) | data formatting | bytes 8388608 | tf_op jit(solution)/shard_map/reshape | solution.py:71
  172.0 1.0 slice_convert_fusion
  173.1 48.0 %all-gather.9.cloned.1.call-done = bf16[2048,2048]{1,0:T(8,128)(2,1)} async-done(((bf16[2048,512]{1,0:T(8,128)(2,1)}), bf16[2048,2048]{1,0:T(8,128)(2,1)}) %all-gather.9.cloned.1.call-update) | async-done | bytes 8388624 | tf_op jit(solution)/shard_map/all_gather | solution.py:70
  221.1 12.4 %fusion.29 = f32[2,2048,512]{2,1,0:T(8,128)S(1)} fusion(bf16[2,2048,512]{2,1,0:T(8,128)(2,1)} %reshape.166, bf16[2048,2048]{1,0:T(8,128)(2,1)} %all-gather.9.cloned.1.call-done), kind=kOutput, calls=%fused_computation.37 | convolution fusion | flops 8589934592 | bytes 20971520 | tf_op jit(solution)/shard_map/td,edf->etf/dot_general | solution.py:72
  233.6 2.2 multiply_convert_fusion
  236.0 59.3 %all-gather.11.cloned.1.call-done = bf16[2,2048,1024]{2,1,0:T(8,128)(2,1)} async-done(((bf16[2,2048,256]{2,1,0:T(8,128)(2,1)}), bf16[2,2048,1024]{2,1,0:T(8,128)(2,1)}) %all-gather.11.cloned.1.call-update) | async-done | bytes 8388624 | tf_op jit(solution)/shard_map/all_gather | solution.py:76
  295.3 9.1 %bitcast_convert_fusion = bf16[2048,512]{1,0:T(8,128)(2,1)} fusion(bf16[2,2048,1024]{2,1,0:T(8,128)(2,1)} %all-gather.11.cloned.1.call-done, bf16[2,1024,512]{2,1,0:T(8,128)(2,1)S(1)} %copy-done.5), kind=kOutput, calls=%fused_computation.40 | convolution fusion | flops 4296015872 | bytes 12582912 | tf_op jit(solution)/shard_map/etf,efd->td/dot_general | solution.py:77
  304.5 68.0 %reduce-scatter.5.cloned.1.call-done = bf16[256,512]{1,0:T(8,128)(2,1)} async-done(((bf16[2048,512]{1,0:T(8,128)(2,1)}), bf16[256,512]{1,0:T(8,128)(2,1)}) %reduce-scatter.5.cloned.1.call-update) | async-done | bytes 262160 | tf_op jit(solution)/shard_map/reduce_scatter | solution.py:80
  372.5 1.9 multiply_reduce_fusion.2
  374.4 8.9 %copy.103 = bf16[2048,3,512]{0,2,1:T(8,128)(2,1)} copy(bf16[2048,3,512]{2,0,1:T(8,128)(2,1)} %param.33) | data formatting | bytes 12582912 | tf_op args[14]
  383.3 7.1 %all-gather.13.cloned.1.call-done = bf16[256,2048]{1,0:T(8,128)(2,1)} async-done(((bf16[256,512]{1,0:T(8,128)(2,1)}), bf16[256,2048]{1,0:T(8,128)(2,1)}) %all-gather.13.cloned.1.call-update) | async-done | bytes 1048592 | tf_op jit(solution)/shard_map/all_gather | solution.py:219
  390.4 5.1 %fusion.27 = f32[256,3,512]{2,0,1:T(8,128)S(1)} fusion(bf16[2048,3,512]{0,2,1:T(8,128)(2,1)} %copy.103, bf16[256,2048]{1,0:T(8,128)(2,1)} %all-gather.13.cloned.1.call-done), kind=kOutput, calls=%fused_computation.35 | convolution fusion | flops 1610612736 | bytes 8912896 | tf_op jit(solution)/shard_map/dot_general | solution.py:218
  395.5 1.2 copy-done.2
  396.8 5.9 %all-reduce = (f32[256]{0:T(256)S(1)}, f32[256]{0:T(256)S(1)}, f32[256]{0:T(256)S(1)}) all-reduce(f32[256]{0:T(256)S(1)} %get-tuple-element.107, f32[256]{0:T(256)S(1)} %get-tuple-element.142, f32[256]{0:T(256)S(1)} %get-tuple-element.106), channel_id=1, replica_groups=mesh['seq'=8,'tp'=4] {'tp'}, use_global_device_ids=true, to_apply=%region_16.17 | all-reduce | flops 768 | bytes 6144 | tf_op jit(solution)/shard_map/psum | solution.py:225
  402.7 2.4 fusion.40
  (93 shorter events, 7.3 us)
Async XLA Ops:
  7.2 66.5 %copy-start = (bf16[512,2048]{1,0:T(8,128)(2,1)S(1)}, bf16[512,2048]{1,0:T(8,128)(2,1)}, u32[]{:S(2)}) copy-start(bf16[512,2048]{1,0:T(8,128)(2,1)} %param.26) | copy-start | bytes 6291460
  7.2 0.8 copy-start.14
  7.2 2.1 copy-start.6
  7.2 63.4 %all-gather.7.cloned.1.call-start = ((), (), s32[]{:S(2)}) async-start(), calls=%async_computation.2 | async-start | bytes 10485760 | tf_op jit(solution)/shard_map/all_gather | solution.py:155
  7.9 92.5 %reduce-scatter.3.cloned.1.call-start = ((), (), s32[]{:S(2)}) async-start(), calls=%async_computation.3 | async-start | bytes 1310720 | tf_op jit(solution)/shard_map/reduce_scatter | solution.py:198
  51.8 1.6 copy-start.7
  73.6 1.8 copy-start.8
  73.6 1.8 copy-start.9
  73.6 26.8 %copy-start.3 = (bf16[256,512]{1,0:T(8,128)(2,1)S(1)}, bf16[256,512]{1,0:T(8,128)(2,1)}, u32[]{:S(2)}) copy-start(bf16[256,512]{1,0:T(8,128)(2,1)} %param.19) | copy-start | bytes 786436
  73.7 33.7 %copy-start.10 = (f32[512]{0:T(512)S(1)}, f32[512]{0:T(512)}, u32[]{:S(2)}) copy-start(f32[512]{0:T(512)} %param.27) | copy-start | bytes 6148
  75.4 85.7 %all-gather.15.cloned.1.call-start = ((), (), s32[]{:S(2)}) async-start(), calls=%async_computation.8 | async-start | bytes 2506752 | tf_op jit(solution)/shard_map/all_gather | solution.py:64
  109.1 111.9 %all-gather.9.cloned.1.call-start = ((), (), s32[]{:S(2)}) async-start(), calls=%async_computation.4 | async-start | bytes 10485760 | tf_op jit(solution)/shard_map/all_gather | solution.py:70
  164.1 131.2 %all-gather.11.cloned.1.call-start = ((), (), s32[]{:S(2)}) async-start(), calls=%async_computation.5 | async-start | bytes 10485760 | tf_op jit(solution)/shard_map/all_gather | solution.py:76
  235.7 59.6 %copy-start.5 = (bf16[2,1024,512]{2,1,0:T(8,128)(2,1)S(1)}, bf16[2,1024,512]{2,1,0:T(8,128)(2,1)}, u32[]{:S(2)}) copy-start(bf16[2,1024,512]{2,1,0:T(8,128)(2,1)} %constant_dynamic-slice_fusion) | copy-start | bytes 6291460
  235.8 136.7 %reduce-scatter.5.cloned.1.call-start = ((), (), s32[]{:S(2)}) async-start(), calls=%async_computation.6 | async-start | bytes 2359296 | tf_op jit(solution)/shard_map/reduce_scatter | solution.py:80
  304.4 68.0 %copy-start.4 = (bf16[256,512]{1,0:T(8,128)(2,1)S(1)}, bf16[256,512]{1,0:T(8,128)(2,1)}, u32[]{:S(2)}) copy-start(bf16[256,512]{1,0:T(8,128)(2,1)} %reduce-scatter.3.cloned.1.call-done) | copy-start | bytes 786436
  304.4 68.0 %copy-start.11 = (f32[512]{0:T(512)S(1)}, f32[512]{0:T(512)}, u32[]{:S(2)}) copy-start(f32[512]{0:T(512)} %param.32) | copy-start | bytes 6148
  304.5 86.0 %all-gather.13.cloned.1.call-start = ((), (), s32[]{:S(2)}) async-start(), calls=%async_computation.7 | async-start | bytes 1310720 | tf_op jit(solution)/shard_map/all_gather | solution.py:219
  383.3 19.4 %copy-start.12 = (f32[512]{0:T(512)S(1)}, f32[512]{0:T(512)}, u32[]{:S(2)}) copy-start(f32[512]{0:T(512)} %param.35) | copy-start | bytes 6148
  383.3 19.4 %copy-start.13 = (f32[512]{0:T(512)S(1)}, f32[512]{0:T(512)}, u32[]{:S(2)}) copy-start(f32[512]{0:T(512)} %param.34) | copy-start | bytes 6148
  390.4 14.7 %copy-start.1 = (bf16[512,2048]{1,0:T(8,128)(2,1)S(1)}, bf16[512,2048]{1,0:T(8,128)(2,1)}, u32[]{:S(2)}) copy-start(bf16[512,2048]{1,0:T(8,128)(2,1)} %param.26) | copy-start | bytes 6291460
  395.5 1.2 copy-start.2
Sparse Core Ops, SparseCore 0:
  9.6 60.9 all-gather.6
  75.5 24.8 reduce-scatter.2
  109.3 51.7 all-gather.14
  164.3 56.7 all-gather.8
  235.9 59.3 all-gather.10
  304.6 67.8 reduce-scatter.4
  374.7 15.6 all-gather.12
where the time goes:
time: 414 us; the launch traced here: 412 us
  waiting for transfers between devices  276 us (67%)
  matrix products  50.8 us (12%)
  local copies, waits for them, and re-layouts  38.4 us (9%)
  other arithmetic  19.2 us (5%)
  between operations  15.1 us (4%)
  blocking collectives  11.7 us (3%)
    reduce_scatter x1, waiting for transfers between devices, dense_experts(): partial = lax.psum_scatter(partial, 'seq', scatter_dimension=0, tiled=True)  68 us
    all_gather x1, waiting for transfers between devices, dense_experts(): weighted = lax.all_gather(weighted, 'tp', axis=2, tiled=True)  59.3 us
    all_gather x1, waiting for transfers between devices, dense_experts(): gathered = lax.all_gather(packed, 'seq', axis=0, tiled=False)  51.9 us
    all_gather x1, waiting for transfers between devices, dense_experts(): rows = lax.all_gather(rows_q, 'tp', axis=1, tiled=True)  48 us
    reduce_scatter x1, waiting for transfers between devices, body(): lax.psum_scatter(attn_term.astype(jnp.bfloat16), 'tp', scatter_dimension=...  24.9 us
    unnamed x35, local copies, waits for them, and re-layouts  23.3 us
    all_gather x1, waiting for transfers between devices, body(): down_full = lax.all_gather(expert_down, 'tp', axis=1, tiled=True)  16.1 us
    dot_general x1, matrix products, dense_experts(): jnp.einsum('td,edf->etf', rows, gate_up, preferred_element_type=jnp.float32)  12.4 us
  transfers between devices with their start and end apart: 7, of which 7 were waited for; matrix products, arithmetic and copies ran while one was open for 15% of the time, Pallas kernels for 0%

commit v1 on v0

--- a/solution.py
+++ b/solution.py
@@ -73,7 +73,14 @@
     activated = jax.nn.silu(projected[..., :hidden_quarter]) * projected[..., hidden_quarter:]
     activated = activated.astype(jnp.bfloat16).astype(jnp.float32)
     weighted = (activated * gate_local[:, :, None]).astype(jnp.bfloat16)
-    weighted = lax.all_gather(weighted, "tp", axis=2, tiled=True)
+    count = lax.axis_size("tp")
+    hops = [(i, (i + 1) % count) for i in range(count)]
+    parts = [weighted]
+    for hop in range(1, count):
+        parts = [lax.ppermute(parts[0], "tp", hops), *parts]
+    whole = jnp.concatenate(parts, axis=2)
+    turn = (lax.axis_index("tp") + 1) * parts[-1].shape[2]
+    weighted = jnp.roll(whole, turn, axis=2)
     partial = jnp.einsum(
         "etf,efd->td", weighted, down_full, preferred_element_type=jnp.float32
     ).astype(jnp.bfloat16)

time: 414 us -> 440 us (1.063)
  local copies, waits for them, and re-layouts: 38.4 us -> 53 us
  waiting for transfers between devices: 276 us -> 288 us
    ppermute x0 -> x3, waiting for transfers between devices: none -> 76.5 us  [dense_experts(): parts = [lax.ppermute(parts[0], 'tp', hops), *parts]]
    all_gather x1 -> x0, waiting for transfers between devices: 59.3 us -> none  [dense_experts(): weighted = lax.all_gather(weighted, 'tp', axis=2, tiled=True)]
    unnamed x35 -> x41, local copies, waits for them, and re-layouts: 23.3 us -> 33.5 us
  transfers between devices with their start and end apart: 7 -> 9, of which waited for: 7 -> 9; matrix products, arithmetic and copies ran while one was open for 15% -> 16% of each run, Pallas kernels for 0% -> 0%
where the time goes in v1:
time: 440 us; the launch traced here: 438 us
  waiting for transfers between devices  288 us (65%)
  local copies, waits for them, and re-layouts  53 us (12%)
  matrix products  48.4 us (11%)
  other arithmetic  21 us (5%)
  between operations  15.2 us (3%)
  blocking collectives  11.7 us (3%)
    ppermute x3, waiting for transfers between devices, dense_experts(): parts = [lax.ppermute(parts[0], 'tp', hops), *parts]  76.5 us
    reduce_scatter x1, waiting for transfers between devices, dense_experts(): partial = lax.psum_scatter(partial, 'seq', scatter_dimension=0, tiled=True)  67.9 us
    all_gather x1, waiting for transfers between devices, dense_experts(): gathered = lax.all_gather(packed, 'seq', axis=0, tiled=False)  51.9 us
    all_gather x1, waiting for transfers between devices, dense_experts(): rows = lax.all_gather(rows_q, 'tp', axis=1, tiled=True)  44.3 us
    unnamed x41, local copies, waits for them, and re-layouts  33.5 us
    reduce_scatter x1, waiting for transfers between devices, body(): lax.psum_scatter(attn_term.astype(jnp.bfloat16), 'tp', scatter_dimension=...  24.9 us
    all_gather x1, waiting for transfers between devices, body(): down_full = lax.all_gather(expert_down, 'tp', axis=1, tiled=True)  14.5 us
    dot_general x1, matrix products, dense_experts(): jnp.einsum('td,edf->etf', rows, gate_up, preferred_element_type=jnp.float32)  12.5 us
  transfers between devices with their start and end apart: 9, of which 9 were waited for; matrix products, arithmetic and copies ran while one was open for 16% of the time, Pallas kernels for 0%

profile of v1, /device:TPU:0, one launch (start us, length us, event | category | flops | bytes accessed | tf_op | source)
XLA Modules:
  0.0 438.0 jit_solution(4071946349274324740)
XLA Ops:
  8.0 1.2 dynamic_slice.22
  9.9 6.4 %copy.105 = bf16[1,4096,512]{1,2,0:T(8,128)(2,1)} copy(bf16[1,4096,512]{2,1,0:T(8,128)(2,1)} %param.23) | data formatting | bytes 8388608 | tf_op args[4]
  16.7 6.6 %copy.107 = bf16[1,4096,512]{1,2,0:T(8,128)(2,1)} copy(bf16[1,4096,512]{2,1,0:T(8,128)(2,1)} %param.24) | data formatting | bytes 8388608 | tf_op args[5]
  23.3 28.9 %while.14 = (s32[]{:T(128)}, f32[1,256,4,128]{1,3,2,0:T(8,128)S(1)}, f32[1,256,4]{1,2,0:T(4,128)S(1)}, f32[1,256,4]{1,2,0:T(4,128)S(1)}, s32[]{:T(128)}, /*index...) while((s32[]{:T(128)}, ...), condition=%wide.region_4.5_spmd, body=%wide.region_1.4_spmd.sunk | while | flops 275651584 | bytes 8731331 | solution.py:195
  24.0 1.6 bitcast_reduce_fusion.2
  26.3 1.8 fusion.87
  28.9 1.6 bitcast_reduce_fusion.2
  31.1 1.8 fusion.87
  33.7 1.6 bitcast_reduce_fusion.2
  35.9 1.9 fusion.87
  38.5 1.6 bitcast_reduce_fusion.2
  40.8 1.8 fusion.87
  43.3 1.6 bitcast_reduce_fusion.2
  45.6 1.8 fusion.87
  48.1 1.6 bitcast_reduce_fusion.2
  50.4 1.8 fusion.87
  52.5 1.3 fusion.68
  54.0 1.4 convolution_bitcast_fusion.1
  56.1 14.5 %all-gather.6.cloned.1.call-done = bf16[2,1024,2048]{2,1,0:T(8,128)(2,1)} async-done(((bf16[2,256,2048]{2,1,0:T(8,128)(2,1)}), bf16[2,1024,2048]{2,1,0:T(8,128)(2,1)}) %all-gather.6.cloned.1.call-update) | async-done | bytes 8388624 | tf_op jit(solution)/shard_map/all_gather | solution.py:162
  70.6 3.0 constant_dynamic-slice_fusion
  73.6 1.7 convolution_convert_fusion
  75.5 24.9 %reduce-scatter.3.cloned.1.call-done = bf16[256,512]{1,0:T(8,128)(2,1)} async-done(((bf16[256,2048]{1,0:T(8,128)(2,1)}), bf16[256,512]{1,0:T(8,128)(2,1)}) %reduce-scatter.3.cloned.1.call-update) | async-done | bytes 262160 | tf_op jit(solution)/shard_map/reduce_scatter | solution.py:205
  101.5 5.8 %psum.28 = f32[256]{0:T(256)S(1)} all-reduce(f32[256]{0:T(256)S(1)} %multiply_reduce_fusion.3), channel_id=1, replica_groups=mesh['seq'=8,'tp'=4] {'tp'}, use_global_device_ids=true, to_apply=%region_10.11 | all-reduce | flops 256 | bytes 2048 | tf_op jit(solution)/shard_map/psum | solution.py:208
  109.2 51.9 %all-gather.12.cloned.1.call-done = bf16[2176,512]{1,0:T(8,128)(2,1)} async-done(((bf16[272,512]{1,0:T(8,128)(2,1)}), bf16[2176,512]{1,0:T(8,128)(2,1)}) %all-gather.12.cloned.1.call-update) | async-done | bytes 2228240 | tf_op jit(solution)/shard_map/all_gather | solution.py:64
  161.0 3.1 slice.40
  164.1 11.5 %copy.120 = bf16[2,2048,2,256]{1,3,2,0:T(8,128)(2,1)} copy(bf16[2,2048,2,256]{3,2,1,0:T(2,128)(2,1)} %param.30) | data formatting | bytes 8388608 | tf_op jit(solution)/shard_map/reshape | solution.py:71
  176.7 44.3 %all-gather.8.cloned.1.call-done = bf16[2048,2048]{1,0:T(8,128)(2,1)} async-done(((bf16[2048,512]{1,0:T(8,128)(2,1)}), bf16[2048,2048]{1,0:T(8,128)(2,1)}) %all-gather.8.cloned.1.call-update) | async-done | bytes 8388624 | tf_op jit(solution)/shard_map/all_gather | solution.py:70
  221.1 12.5 %fusion.31 = f32[2,2048,512]{1,2,0:T(8,128)S(1)} fusion(bf16[2,2048,512]{1,2,0:T(8,128)(2,1)} %bitcast.166, bf16[2048,2048]{1,0:T(8,128)(2,1)} %all-gather.8.cloned.1.call-done), kind=kOutput, calls=%fused_computation.39 | convolution fusion | flops 8589934592 | bytes 20971520 | tf_op jit(solution)/shard_map/td,edf->etf/dot_general | solution.py:72
  233.6 1.4 multiply_convert_fusion
  235.0 1.8 copy-done.2
  237.1 25.2 %collective-permute-done = bf16[2,2048,256]{1,2,0:T(8,128)(2,1)S(1)} collective-permute-done((bf16[2,2048,256]{1,2,0:T(8,128)(2,1)S(1)}, bf16[2,2048,256]{1,2,0:T(8,128)(2,1)S(1)}, u32[]{:S(2)}, u32[]{:S(2)}) %collective-permute-start) | collective-permute-done | bytes 2097184 | tf_op jit(solution)/shard_map/ppermute | solution.py:80
  262.3 25.6 %collective-permute-done.1 = bf16[2,2048,256]{1,2,0:T(8,128)(2,1)} collective-permute-done((bf16[2,2048,256]{1,2,0:T(8,128)(2,1)S(1)}, bf16[2,2048,256]{1,2,0:T(8,128)(2,1)}, u32[]{:S(2)}, u32[]{:S(2)}) %collective-permute-start.1) | collective-permute-done | bytes 2097184 | tf_op jit(solution)/shard_map/ppermute | solution.py:80
  287.9 25.8 %collective-permute-done.2 = bf16[2,2048,256]{1,2,0:T(8,128)(2,1)} collective-permute-done((bf16[2,2048,256]{1,2,0:T(8,128)(2,1)}, bf16[2,2048,256]{1,2,0:T(8,128)(2,1)}, u32[]{:S(2)}, u32[]{:S(2)}) %collective-permute-start.2) | collective-permute-done | bytes 2097184 | tf_op jit(solution)/shard_map/ppermute | solution.py:80
  313.6 1.9 constant_dynamic-update-slice_fusion.7
  315.5 2.0 constant_dynamic-update-slice_fusion.6
  318.3 1.4 constant_dynamic-update-slice_fusion.4
  319.6 1.7 constant_dynamic-update-slice_fusion.3
  321.4 1.7 constant_dynamic-update-slice_fusion.2
  323.3 1.4 constant_dynamic-update-slice_fusion
  324.8 5.8 %bitcast_convert_fusion = bf16[2048,512]{1,0:T(8,128)(2,1)} fusion(bf16[2,1024,512]{2,1,0:T(8,128)(2,1)S(1)} %copy-done.7, bf16[2,2048,2048]{1,2,0:T(8,128)(2,1)S(1)} %constant_dynamic-update-slice_fusion, s32[]{:T(128)S(6)} %select_n.59), kind=kOutput, calls=%fused_computation.42 | convolution fusion | flops 4296015872 | bytes 12582916 | tf_op jit(solution)/shard_map/etf,efd->td/dot_general | solution.py:84
  330.7 67.9 %reduce-scatter.5.cloned.1.call-done = bf16[256,512]{1,0:T(8,128)(2,1)} async-done(((bf16[2048,512]{1,0:T(8,128)(2,1)}), bf16[256,512]{1,0:T(8,128)(2,1)}) %reduce-scatter.5.cloned.1.call-update) | async-done | bytes 262160 | tf_op jit(solution)/shard_map/reduce_scatter | solution.py:87
  398.6 1.9 multiply_reduce_fusion.2
  400.5 8.9 %copy.115 = bf16[2048,3,512]{0,2,1:T(8,128)(2,1)} copy(bf16[2048,3,512]{2,0,1:T(8,128)(2,1)} %param.33) | data formatting | bytes 12582912 | tf_op args[14]
  409.4 7.0 %all-gather.10.cloned.1.call-done = bf16[256,2048]{1,0:T(8,128)(2,1)} async-done(((bf16[256,512]{1,0:T(8,128)(2,1)}), bf16[256,2048]{1,0:T(8,128)(2,1)}) %all-gather.10.cloned.1.call-update) | async-done | bytes 1048592 | tf_op jit(solution)/shard_map/all_gather | solution.py:226
  416.4 5.1 %fusion.29 = f32[256,3,512]{2,0,1:T(8,128)S(1)} fusion(bf16[2048,3,512]{0,2,1:T(8,128)(2,1)} %copy.115, bf16[256,2048]{1,0:T(8,128)(2,1)} %all-gather.10.cloned.1.call-done), kind=kOutput, calls=%fused_computation.37 | convolution fusion | flops 1610612736 | bytes 8912896 | tf_op jit(solution)/shard_map/dot_general | solution.py:225
  421.5 1.2 copy-done.4
  422.8 5.9 %all-reduce = (f32[256]{0:T(256)S(1)}, f32[256]{0:T(256)S(1)}, f32[256]{0:T(256)S(1)}) all-reduce(f32[256]{0:T(256)S(1)} %get-tuple-element.107, f32[256]{0:T(256)S(1)} %get-tuple-element.142, f32[256]{0:T(256)S(1)} %get-tuple-element.106), channel_id=1, replica_groups=mesh['seq'=8,'tp'=4] {'tp'}, use_global_device_ids=true, to_apply=%region_16.17 | all-reduce | flops 768 | bytes 6144 | tf_op jit(solution)/shard_map/psum | solution.py:232
  428.7 2.4 fusion.44
  (104 shorter events, 15.8 us)
Async XLA Ops:
  7.2 66.5 %copy-start = (bf16[512,2048]{1,0:T(8,128)(2,1)S(1)}, bf16[512,2048]{1,0:T(8,128)(2,1)}, u32[]{:S(2)}) copy-start(bf16[512,2048]{1,0:T(8,128)(2,1)} %param.26) | copy-start | bytes 6291460
  7.2 63.4 %all-gather.6.cloned.1.call-start = ((), (), s32[]{:S(2)}) async-start(), calls=%async_computation.2 | async-start | bytes 10485760 | tf_op jit(solution)/shard_map/all_gather | solution.py:162
  7.9 92.5 %reduce-scatter.3.cloned.1.call-start = ((), (), s32[]{:S(2)}) async-start(), calls=%async_computation.3 | async-start | bytes 1310720 | tf_op jit(solution)/shard_map/reduce_scatter | solution.py:205
  9.9 6.5 %copy-start.8 = (bf16[256,512]{1,0:T(8,128)(2,1)S(1)}, bf16[256,512]{1,0:T(8,128)(2,1)}, u32[]{:S(2)}) copy-start(bf16[256,512]{1,0:T(8,128)(2,1)} %param.20) | copy-start | bytes 786436
  56.1 19.3 %copy-start.9 = (f32[256,8]{0,1:T(8,128)S(1)}, f32[256,8]{0,1:T(8,128)}, u32[]{:S(2)}) copy-start(f32[256,8]{0,1:T(8,128)} %param.29) | copy-start | bytes 24580
  56.1 19.3 %copy-start.10 = (s32[256,8]{0,1:T(8,128)S(1)}, s32[256,8]{0,1:T(8,128)}, u32[]{:S(2)}) copy-start(s32[256,8]{0,1:T(8,128)} %param.28) | copy-start | bytes 24580
  56.1 44.3 %copy-start.5 = (bf16[256,512]{1,0:T(8,128)(2,1)S(1)}, bf16[256,512]{1,0:T(8,128)(2,1)}, u32[]{:S(2)}) copy-start(bf16[256,512]{1,0:T(8,128)(2,1)} %param.19) | copy-start | bytes 786436
  56.1 51.2 %copy-start.11 = (f32[512]{0:T(512)S(1)}, f32[512]{0:T(512)}, u32[]{:S(2)}) copy-start(f32[512]{0:T(512)} %param.27) | copy-start | bytes 6148
  75.3 85.7 %all-gather.12.cloned.1.call-start = ((), (), s32[]{:S(2)}) async-start(), calls=%async_computation.7 | async-start | bytes 2506752 | tf_op jit(solution)/shard_map/all_gather | solution.py:64
  109.1 111.9 %all-gather.8.cloned.1.call-start = ((), (), s32[]{:S(2)}) async-start(), calls=%async_computation.4 | async-start | bytes 10485760 | tf_op jit(solution)/shard_map/all_gather | solution.py:70
  164.1 234.5 %reduce-scatter.5.cloned.1.call-start = ((), (), s32[]{:S(2)}) async-start(), calls=%async_computation.5 | async-start | bytes 2359296 | tf_op jit(solution)/shard_map/reduce_scatter | solution.py:87
  233.6 3.2 copy-start.2
  236.8 25.5 %collective-permute-start = (bf16[2,2048,256]{1,2,0:T(8,128)(2,1)S(1)}, bf16[2,2048,256]{1,2,0:T(8,128)(2,1)S(1)}, u32[]{:S(2)}, u32[]{:S(2)}) collective-permute-start(bf16[2,2048,256]{1,2,0:T(8,128)(2,1)S(1)} %multiply_convert_fusion), channel_id=1, source_target_pairs={{0,1},{1,2},{2,3},{3,0},{4,5},{5,6},{6,7},{7,4},{8,9},{9,10},{10,1... | collective-permute-start | bytes 6291464 | tf_op jit(solution)/shard_map/ppermute | solution.py:80
  262.3 25.6 %collective-permute-start.1 = (bf16[2,2048,256]{1,2,0:T(8,128)(2,1)S(1)}, bf16[2,2048,256]{1,2,0:T(8,128)(2,1)}, u32[]{:S(2)}, u32[]{:S(2)}) collective-permute-start(bf16[2,2048,256]{1,2,0:T(8,128)(2,1)S(1)} %collective-permute-done), channel_id=1, source_target_pairs={{0,1},{1,2},{2,3},{3,0},{4,5},{5,6},{6,7},{7,4},{8,9},{9,10},{10,1... | collective-permute-start | bytes 6291464 | tf_op jit(solution)/shard_map/ppermute | solution.py:80
  287.8 25.8 %collective-permute-start.2 = (bf16[2,2048,256]{1,2,0:T(8,128)(2,1)}, bf16[2,2048,256]{1,2,0:T(8,128)(2,1)}, u32[]{:S(2)}, u32[]{:S(2)}) collective-permute-start(bf16[2,2048,256]{1,2,0:T(8,128)(2,1)} %collective-permute-done.1), channel_id=1, source_target_pairs={{0,1},{1,2},{2,3},{3,0},{4,5},{5,6},{6,7},{7,4},{8,9},{9,10},{10,1... | collective-permute-start | bytes 6291464 | tf_op jit(solution)/shard_map/ppermute | solution.py:80
  313.6 4.6 %copy-start.3 = (f32[2,2048,512]{1,2,0:T(8,128)S(1)}, f32[2,2048,512]{1,2,0:T(8,128)}, u32[]{:S(2)}) copy-start(f32[2,2048,512]{1,2,0:T(8,128)} %copy-done.2) | copy-start | bytes 25165828
  323.2 1.6 copy-start.7
  324.8 73.8 %copy-start.6 = (bf16[256,512]{1,0:T(8,128)(2,1)S(1)}, bf16[256,512]{1,0:T(8,128)(2,1)}, u32[]{:S(2)}) copy-start(bf16[256,512]{1,0:T(8,128)(2,1)} %reduce-scatter.3.cloned.1.call-done) | copy-start | bytes 786436
  324.8 73.8 %copy-start.12 = (f32[512]{0:T(512)S(1)}, f32[512]{0:T(512)}, u32[]{:S(2)}) copy-start(f32[512]{0:T(512)} %param.32) | copy-start | bytes 6148
  330.6 85.8 %all-gather.10.cloned.1.call-start = ((), (), s32[]{:S(2)}) async-start(), calls=%async_computation.6 | async-start | bytes 1310720 | tf_op jit(solution)/shard_map/all_gather | solution.py:226
  409.4 19.3 %copy-start.13 = (f32[512]{0:T(512)S(1)}, f32[512]{0:T(512)}, u32[]{:S(2)}) copy-start(f32[512]{0:T(512)} %param.35) | copy-start | bytes 6148
  409.4 19.3 %copy-start.14 = (f32[512]{0:T(512)S(1)}, f32[512]{0:T(512)}, u32[]{:S(2)}) copy-start(f32[512]{0:T(512)} %param.34) | copy-start | bytes 6148
  416.4 14.7 %copy-start.1 = (bf16[512,2048]{1,0:T(8,128)(2,1)S(1)}, bf16[512,2048]{1,0:T(8,128)(2,1)}, u32[]{:S(2)}) copy-start(bf16[512,2048]{1,0:T(8,128)(2,1)} %param.26) | copy-start | bytes 6291460
  421.5 1.2 copy-start.4
Sparse Core Ops, SparseCore 0:
  9.6 60.9 all-gather.5
  75.5 24.8 reduce-scatter.2
  109.2 51.7 all-gather.11
  164.2 56.7 all-gather.7
  330.7 67.8 reduce-scatter.4
  400.7 15.6 all-gather.9
